TPU v7x, 512 devices: a whole 4x4x16 slice. The times are simulated.
512 devices in a mesh: dp: 8 (over x, core), tensor: 64 (over z, y).
Axes of the slice: x: 4, y: 4, z: 16, core: 2. Of those that a mesh axis runs over, the one named last changes fastest.
Arguments:
- states: bfloat16 [65536, 2048], P(('dp', 'tensor')), may hold values from -150 to 150
- norm_gain: float32 [2048], replicated, may hold values from 0.1 to 1.9
- norm_bias: float32 [2048], replicated, may hold values from -3 to 3
- head_table: bfloat16 [250880, 2048], P('tensor', 'dp'), may hold values from -2 to 2
- seq_lengths: int32 [8], P('dp'), may hold values from 4096 to 8192
- scored_index: int32 [2048], P('dp'), may hold values from 0 to 8191
- targets: int32 [2048], P('dp'), may hold values from 0 to 250879
- slot_mask: int32 [2048], P('dp'), may hold values 0 or 1
Outputs:
- logprob: float32 [2048], P(('dp', 'tensor'))
- entropy: float32 [2048], P(('dp', 'tensor'))
All inputs are finite; a program needn't handle non-finite values. No bound on the sum of `slot_mask` on one device may be relied on, other than what follows from the above.
Results may differ from a plain program's by a relative error of at most 0.012.
The roundings to bfloat16 on the way count: a program that leaves them out, or rounds other values in their place, can miss the bound.
Values may be sent and summed in bfloat16 or wider, within the bound.
No kernel may reach another device: no remote copies, remote signals or barrier semaphores. Data moves between devices by JAX's collectives and lax.ppermute only.
A program may use at most 64 MiB of HBM per device.

v0:
```python
import jax
import jax.numpy as jnp
from jax import lax
from jax.sharding import Mesh, PartitionSpec as P

EPSILON = 1e-05
TENSOR = ("tz", "ty")


def layer_norm(states, norm_gain, norm_bias):
    values = states.astype(jnp.float32)
    center = jnp.mean(values, axis=1, keepdims=True)
    shifted = values - center
    variance = jnp.mean(shifted * shifted, axis=1, keepdims=True)
    return (shifted * lax.rsqrt(variance + EPSILON) * norm_gain + norm_bias).astype(jnp.bfloat16)


def contract_last(left, right):
    return lax.dot_general(
        left, right, (((1,), (1,)), ((), ())), preferred_element_type=jnp.float32
    )


def body(states, norm_gain, norm_bias, head_table, seq_lengths, scored_index, targets, slot_mask):
    local_rows = states.shape[0]
    devices = lax.axis_size(TENSOR)
    position = lax.axis_index(TENSOR)
    first_row = position * local_rows
    scored_count = scored_index.shape[0]
    owned_count = scored_count // devices
    offset = position * owned_count
    width = states.shape[1]
    row_iota = jnp.arange(local_rows, dtype=jnp.int32)
    picker = (scored_index[:, None] - first_row == row_iota[None, :]).astype(jnp.bfloat16)
    picked = jnp.dot(picker, states, preferred_element_type=jnp.float32).astype(jnp.bfloat16)
    ring = lax.axis_size("ty")
    by_y = picked.reshape(devices // ring, ring, owned_count, width).transpose(1, 0, 2, 3)
    near = lax.all_to_all(by_y, "ty", 0, 0, tiled=True)
    near = jnp.sum(near.astype(jnp.float32), axis=0).astype(jnp.bfloat16)
    arrived = lax.all_to_all(near, "tz", 0, 0, tiled=True)
    owned_rows = jnp.sum(arrived.astype(jnp.float32), axis=0)
    owned_normed = layer_norm(owned_rows, norm_gain, norm_bias)
    along_z = lax.all_to_all(
        jnp.broadcast_to(owned_normed[None], (devices // ring, owned_count, width)),
        "tz",
        0,
        0,
        tiled=True,
    )
    along_y = lax.all_to_all(
        jnp.broadcast_to(along_z[None], (ring, devices // ring, owned_count, width)),
        "ty",
        0,
        0,
        tiled=True,
    )
    chosen = along_y.transpose(1, 0, 2, 3).reshape(scored_count, width)
    vocab_local = head_table.shape[0]
    split = vocab_local // 32 * 16
    local_target = targets - position * vocab_local
    parts = []
    for low, high in ((0, split), (split, vocab_local)):
        logits = contract_last(
            chosen, lax.all_gather(head_table[low:high], "dp", axis=1, tiled=True)
        )
        vocab_iota = jnp.arange(low, high, dtype=jnp.int32)
        target_hits = local_target[:, None] == vocab_iota[None, :]
        part_maxima = jnp.max(logits, axis=1)
        shifted = logits - part_maxima[:, None]
        weights = jnp.exp(shifted)
        parts.append(
            jnp.stack(
                [
                    part_maxima,
                    jnp.sum(weights, axis=1),
                    jnp.sum(weights * shifted, axis=1),
                    jnp.sum(jnp.where(target_hits, logits, 0.0), axis=1),
                ],
                axis=1,
            )
        )
    stats = jnp.stack(parts, axis=1)
    gathered = lax.all_to_all(stats.reshape(devices, owned_count, 2, 4), TENSOR, 0, 0, tiled=True)
    gathered = gathered.transpose(0, 2, 1, 3).reshape(devices * 2, owned_count, 4)
    part_max = gathered[:, :, 0]
    maxima = jnp.max(part_max, axis=0)
    gap = part_max - maxima[None, :]
    scale = jnp.exp(gap)
    totals = jnp.sum(scale * gathered[:, :, 1], axis=0)
    weighted = jnp.sum(scale * (gathered[:, :, 2] + gap * gathered[:, :, 1]), axis=0)
    target_logit = jnp.sum(gathered[:, :, 3], axis=0)
    own_index = lax.dynamic_slice_in_dim(scored_index, offset, owned_count)
    own_mask = lax.dynamic_slice_in_dim(slot_mask, offset, owned_count)
    segment = local_rows * devices // seq_lengths.shape[0]
    sequence = own_index // segment
    seq_iota = jnp.arange(seq_lengths.shape[0], dtype=jnp.int32)
    length_of = jnp.sum(
        jnp.where(sequence[:, None] == seq_iota[None, :], seq_lengths[None, :], 0), axis=1
    )
    live_slot = (own_mask == 1) & (own_index % segment < length_of)
    log_total = jnp.log(totals)
    logprob = jnp.where(live_slot, target_logit - maxima - log_total, 0.0)
    entropy = jnp.where(live_slot, log_total - weighted / totals, 0.0)
    return (logprob, entropy)


def split_mesh(mesh):
    grid = mesh.devices
    first = grid[0]
    coords = [getattr(d, "coords", None) for d in first]
    ring = len({c[1] for c in coords}) if all((c is not None for c in coords)) else 1
    return Mesh(grid.reshape(grid.shape[0], grid.shape[1] // ring, ring), ("dp", "tz", "ty"))


def solution(mesh):
    return jax.shard_map(
        body,
        mesh=split_mesh(mesh),
        in_specs=(
            P(("dp", "tz", "ty"), None),
            P(),
            P(),
            P(("tz", "ty"), "dp"),
            P("dp"),
            P("dp"),
            P("dp"),
            P("dp"),
        ),
        out_specs=(P(("dp", "tz", "ty")), P(("dp", "tz", "ty"))),
        check_vma=False,
    )
```

profile of v0, /device:TPU:2, one launch (start us, length us, event | category | flops | bytes accessed | tf_op | source)
XLA Modules:
  0.0 195.1 jit_solution(13988544709984714789)
XLA Ops:
  7.2 2.4 %slice.19 = bf16[1952,256]{1,0:T(8,128)(2,1)} slice(bf16[3920,256]{1,0:T(8,128)(2,1)} %param.11), slice={[0:1952], [0:256]} | slice | bytes 1998848 | tf_op jit(solution)/shard_map/slice | solution.py:64
  9.7 1.0 slice.20
  10.8 0.5 convolution_convert_fusion
  12.2 19.4 %all_to_all.25 = bf16[4,16,4,2048]{3,2,1,0:T(4,128)(2,1)S(1)} all-to-all(bf16[4,16,4,2048]{3,2,1,0:T(4,128)(2,1)S(1)} %bitcast.15), channel_id=1, replica_groups=mesh['dp'=8,'tz'=16,'ty'=4] {'ty'}, dimensions={0} | all-to-all | bytes 2097152 | tf_op jit(solution)/shard_map/all_to_all | solution.py:38
  31.6 0.7 reduce_sum.124
  32.3 32.5 %all_to_all.26 = bf16[16,4,2048]{2,1,0:T(4,128)(2,1)S(1)} all-to-all(bf16[16,4,2048]{2,1,0:T(4,128)(2,1)S(1)} %reduce_sum.124), channel_id=1, replica_groups=mesh['dp'=8,'tz'=16,'ty'=4] {'tz'}, dimensions={0} | all-to-all | bytes 524288 | tf_op jit(solution)/shard_map/all_to_all | solution.py:40
  65.7 22.5 %all_to_all.27 = bf16[16,4,2048]{2,1,0:T(4,128)(2,1)S(1)} all-to-all(bf16[16,4,2048]{2,1,0:T(4,128)(2,1)S(1)} %broadcast_in_dim.26), channel_id=1, replica_groups=mesh['dp'=8,'tz'=16,'ty'=4] {'tz'}, dimensions={0} | all-to-all | bytes 524288 | tf_op jit(solution)/shard_map/all_to_all | solution.py:43
  88.2 1.5 broadcast_in_dim.27
  89.7 3.5 %all-to-all-start.3 = ((bf16[4,16,4,2048]{3,2,1,0:T(4,128)(2,1)}), bf16[4,16,4,2048]{3,2,1,0:T(4,128)(2,1)S(1)}, u32[]{:S(2)}, u32[]{:S(2)}) async-start(bf16[4,16,4,2048]{3,2,1,0:T(4,128)(2,1)} %broadcast_in_dim.27), calls=%async_computation.3 | async-start | bytes 2097152 | tf_op jit(solution)/shard_map/all_to_all | solution.py:50
  93.2 10.8 %all-to-all-done.3 = bf16[4,16,4,2048]{3,2,1,0:T(4,128)(2,1)S(1)} async-done(((bf16[4,16,4,2048]{3,2,1,0:T(4,128)(2,1)}), bf16[4,16,4,2048]{3,2,1,0:T(4,128)(2,1)S(1)}, u32[]{:S(2)}, u32[]{:S(2)}) %all-to-all-start.3) | async-done | bytes 1048608 | tf_op jit(solution)/shard_map/all_to_all | solution.py:50
  104.0 0.6 copy.56
  104.6 1.1 reshape.126
  105.7 6.0 %fusion.4 = (f32[256]{0:T(256)S(1)}, f32[256,1952]{0,1:T(8,128)S(1)}) fusion(bf16[256,2048]{1,0:T(8,128)(2,1)} %reshape.126, bf16[1952,2048]{1,0:T(8,128)(2,1)} %all-gather.3.cloned.1.call-done), kind=kOutput, calls=%fused_computation.40 | convolution fusion | flops 2047319808 | bytes 11043840 | tf_op jit(solution)/shard_map/dot_general | solution.py:19
  111.9 0.7 exponential_reduce_fusion.1
  113.2 24.7 %all-gather.5.cloned.1.call-done = bf16[1968,2048]{1,0:T(8,128)(2,1)} async-done(((bf16[1968,256]{1,0:T(8,128)(2,1)}), bf16[1968,2048]{1,0:T(8,128)(2,1)}) %all-gather.5.cloned.1.call-update) | async-done | bytes 8060944 | tf_op jit(solution)/shard_map/all_gather | solution.py:64
  137.9 6.1 %fusion.3 = (f32[256]{0:T(256)S(1)}, f32[256,1968]{0,1:T(8,128)S(1)}) fusion(bf16[256,2048]{1,0:T(8,128)(2,1)} %reshape.126, bf16[1968,2048]{1,0:T(8,128)(2,1)} %all-gather.5.cloned.1.call-done), kind=kOutput, calls=%fused_computation.39 | convolution fusion | flops 2064101120 | bytes 11125760 | tf_op jit(solution)/shard_map/dot_general | solution.py:19
  144.1 1.0 exponential_reduce_fusion
  145.8 0.9 copy.65
  146.7 15.6 %all-to-all-start.4 = ((f32[64,4,2,4]{1,3,2,0:T(4,128)}), f32[64,4,2,4]{1,3,2,0:T(4,128)S(1)}, u32[]{:S(2)}, u32[]{:S(2)}) async-start(f32[64,4,2,4]{1,3,2,0:T(4,128)} %copy.65), calls=%async_computation.4 | async-start | bytes 524288 | tf_op jit(solution)/shard_map/all_to_all | solution.py:83
  163.0 22.3 %all-to-all-done.4 = f32[64,4,2,4]{1,3,2,0:T(4,128)S(1)} async-done(((f32[64,4,2,4]{1,3,2,0:T(4,128)}), f32[64,4,2,4]{1,3,2,0:T(4,128)S(1)}, u32[]{:S(2)}, u32[]{:S(2)}) %all-to-all-start.4) | async-done | bytes 8224 | tf_op jit(solution)/shard_map/all_to_all | solution.py:83
  185.3 1.0 copy.66
  186.3 0.6 slice_reduce_fusion
  187.1 0.6 subtract_select_fusion
  187.7 0.5 subtract_select_fusion.1
  (48 shorter events, 3.5 us)
Async XLA Ops:
  7.2 3.7 %copy-start = (bf16[128,2048]{1,0:T(8,128)(2,1)S(1)}, bf16[128,2048]{1,0:T(8,128)(2,1)}, u32[]{:S(2)}) copy-start(bf16[128,2048]{1,0:T(8,128)(2,1)} %param.8) | copy-start | bytes 1572868
  7.2 2.5 %copy-start.1 = (bf16[3920,256]{1,0:T(8,128)(2,1)S(1)}, bf16[3920,256]{1,0:T(8,128)(2,1)}, u32[]{:S(2)}) copy-start(bf16[3920,256]{1,0:T(8,128)(2,1)} %param.11) | copy-start | bytes 6021124
  7.2 98.6 %all-gather.3.cloned.1.call-start = ((), (), s32[]{:S(2)}) async-start(), calls=%async_computation.5 | async-start | bytes 8994816 | tf_op jit(solution)/shard_map/all_gather | solution.py:64
  9.6 1.2 copy-start.4
  9.7 128.2 %all-gather.5.cloned.1.call-start = ((), (), s32[]{:S(2)}) async-start(), calls=%async_computation.6 | async-start | bytes 9068544 | tf_op jit(solution)/shard_map/all_gather | solution.py:64
  12.2 53.3 %copy-start.2 = (f32[2048]{0:T(1024)S(1)}, f32[2048]{0:T(1024)}, u32[]{:S(2)}) copy-start(f32[2048]{0:T(1024)} %param.10) | copy-start | bytes 24580
  12.2 53.3 %copy-start.3 = (f32[2048]{0:T(1024)S(1)}, f32[2048]{0:T(1024)}, u32[]{:S(2)}) copy-start(f32[2048]{0:T(1024)} %param.9) | copy-start | bytes 24580
  65.7 27.5 %copy-start.5 = (s32[256]{0:T(256)S(1)}, s32[256]{0:T(256)}, u32[]{:S(2)}) copy-start(s32[256]{0:T(256)} %param.14) | copy-start | bytes 3076
  89.7 14.4 %all-to-all-start.3 = ((bf16[4,16,4,2048]{3,2,1,0:T(4,128)(2,1)}), bf16[4,16,4,2048]{3,2,1,0:T(4,128)(2,1)S(1)}, u32[]{:S(2)}, u32[]{:S(2)}) async-start(bf16[4,16,4,2048]{3,2,1,0:T(4,128)(2,1)} %broadcast_in_dim.27), calls=%async_computation.3 | async-start | bytes 2097152 | tf_op jit(solution)/shard_map/all_to_all | solution.py:50
  144.1 43.1 %copy-start.6 = (s32[256]{0:T(256)S(1)}, s32[256]{0:T(256)}, u32[]{:S(2)}) copy-start(s32[256]{0:T(256)} %param.15) | copy-start | bytes 3076
  146.7 38.6 %all-to-all-start.4 = ((f32[64,4,2,4]{1,3,2,0:T(4,128)}), f32[64,4,2,4]{1,3,2,0:T(4,128)S(1)}, u32[]{:S(2)}, u32[]{:S(2)}) async-start(f32[64,4,2,4]{1,3,2,0:T(4,128)} %copy.65), calls=%async_computation.4 | async-start | bytes 524288 | tf_op jit(solution)/shard_map/all_to_all | solution.py:83
Sparse Core Ops, SparseCore 0:
  10.1 64.3 all-gather.2
  76.6 61.1 all-gather.4
where the time goes:
time: 196 us; the launch traced here: 195 us
  blocking collectives  74.4 us (38%)
  waiting for transfers between devices  57.8 us (29%)
  starting transfers between devices  19.2 us (10%)
  between operations  15 us (8%)
  matrix products  12.6 us (6%)
  local copies, waits for them, and re-layouts  11 us (6%)
  other arithmetic  5.14 us (3%)
    all_to_all x1, blocking collectives, body(): arrived = lax.all_to_all(near, 'tz', 0, 0, tiled=True)  32.5 us
    all_gather x2, waiting for transfers between devices, body(): lax.all_gather(head_table[low:high], 'dp', axis=1, tiled=True)  24.7 us
    all_to_all x1, blocking collectives, body(): lax.all_to_all(jnp.broadcast_to(owned_normed[None], (devices // ring, own...  22.5 us
    all_to_all x1, waiting for transfers between devices, body(): lax.all_to_all(stats.reshape(devices, owned_count, 2, 4), TENSOR, 0, 0, t...  22.3 us
    all_to_all x1, blocking collectives, body(): near = lax.all_to_all(by_y, 'ty', 0, 0, tiled=True)  19.4 us
    all_to_all x1, starting transfers between devices, body(): lax.all_to_all(stats.reshape(devices, owned_count, 2, 4), TENSOR, 0, 0, t...  15.6 us
    dot_general x2, matrix products, contract_last(): lax.dot_general(left, right, (((1,), (1,)), ((), ())), preferred_element_...  12.1 us
    all_to_all x1, waiting for transfers between devices, body(): lax.all_to_all(jnp.broadcast_to(along_z[None], (ring, devices // ring, ow...  10.8 us
  transfers between devices with their start and end apart: 4, of which 3 were waited for; matrix products, arithmetic and copies ran while one was open for 7% of the time, Pallas kernels for 0%

commit v1 on v0

--- a/solution.py
+++ b/solution.py
@@ -5,6 +5,11 @@
 
 EPSILON = 1e-05
 TENSOR = ("tz", "ty")
+
+
+def place_numbers_on(frame_in, at_axis=1):
+    p_next = jax.lax.all_to_all(jnp.stack([frame_in] * jax.lax.axis_size("dp"), axis=0), "dp", 0, 0)
+    return jnp.concatenate(p_next, axis=at_axis)
 
 
 def layer_norm(states, norm_gain, norm_bias):
@@ -60,9 +65,7 @@
     local_target = targets - position * vocab_local
     parts = []
     for low, high in ((0, split), (split, vocab_local)):
-        logits = contract_last(
-            chosen, lax.all_gather(head_table[low:high], "dp", axis=1, tiled=True)
-        )
+        logits = contract_last(chosen, place_numbers_on(head_table[low:high]))
         vocab_iota = jnp.arange(low, high, dtype=jnp.int32)
         target_hits = local_target[:, None] == vocab_iota[None, :]
         part_maxima = jnp.max(logits, axis=1)

time: 196 us -> 345 us (1.76)
  waiting for transfers between devices: 57.8 us -> 195 us
  local copies, waits for them, and re-layouts: 11 us -> 30.6 us
  between operations: 15 us -> 1.54 us
  starting transfers between devices: 19.2 us -> 25.2 us
    all_to_all x0 -> x2, waiting for transfers between devices: none -> 162 us  [place_numbers_on(): jax.lax.all_to_all(jnp.stack([frame_in] * jax.lax.axis_size('dp'), axis=0...]
    all_gather x2 -> x0, waiting for transfers between devices: 24.7 us -> none  [body(): lax.all_gather(head_table[low:high], 'dp', axis=1, tiled=True)]
    reshape x0 -> x2, local copies, waits for them, and re-layouts: none -> 15.4 us  [place_numbers_on(): return jnp.concatenate(p_next, axis=at_axis)]
    all_to_all x0 -> x2, starting transfers between devices: none -> 11.7 us  [place_numbers_on(): jax.lax.all_to_all(jnp.stack([frame_in] * jax.lax.axis_size('dp'), axis=0...]
    another operation x0 -> x2, local copies, waits for them, and re-layouts: none -> 7.32 us  [place_numbers_on(): jnp.stack([frame_in] * jax.lax.axis_size('dp'), axis=0)]
    all_to_all x1, starting transfers between devices: 15.6 us -> 9.9 us  [body(): lax.all_to_all(stats.reshape(devices, owned_count, 2, 4), TENSOR, 0, 0, t...]
  transfers between devices with their start and end apart: 4 -> 4, of which waited for: 3 -> 4; matrix products, arithmetic and copies ran while one was open for 7% -> 5% of each run, Pallas kernels for 0% -> 0%
where the time goes in v1:
time: 345 us; the launch traced here: 344 us
  waiting for transfers between devices  195 us (57%)
  blocking collectives  74.3 us (22%)
  local copies, waits for them, and re-layouts  30.6 us (9%)
  starting transfers between devices  25.2 us (7%)
  matrix products  11.6 us (3%)
  other arithmetic  5.83 us (2%)
    all_to_all x2, waiting for transfers between devices, place_numbers_on(): jax.lax.all_to_all(jnp.stack([frame_in] * jax.lax.axis_size('dp'), axis=0...  162 us
    all_to_all x1, blocking collectives, body(): arrived = lax.all_to_all(near, 'tz', 0, 0, tiled=True)  32.5 us
    all_to_all x1, blocking collectives, body(): lax.all_to_all(jnp.broadcast_to(owned_normed[None], (devices // ring, own...  22.5 us
    all_to_all x1, waiting for transfers between devices, body(): lax.all_to_all(stats.reshape(devices, owned_count, 2, 4), TENSOR, 0, 0, t...  21.7 us
    all_to_all x1, blocking collectives, body(): near = lax.all_to_all(by_y, 'ty', 0, 0, tiled=True)  19.4 us
    reshape x2, local copies, waits for them, and re-layouts, place_numbers_on(): return jnp.concatenate(p_next, axis=at_axis)  15.4 us
    all_to_all x2, starting transfers between devices, place_numbers_on(): jax.lax.all_to_all(jnp.stack([frame_in] * jax.lax.axis_size('dp'), axis=0...  11.7 us
    dot_general x2, matrix products, contract_last(): lax.dot_general(left, right, (((1,), (1,)), ((), ())), preferred_element_...  11.2 us
  transfers between devices with their start and end apart: 4, of which 4 were waited for; matrix products, arithmetic and copies ran while one was open for 5% of the time, Pallas kernels for 0%

profile of v1, /device:TPU:2, one launch (start us, length us, event | category | flops | bytes accessed | tf_op | source)
XLA Modules:
  0.0 344.2 jit_solution(10715193880713658785)
XLA Ops:
  0.7 0.7 broadcast_subtract_fusion.1
  3.1 19.4 %all_to_all.35 = bf16[4,16,4,2048]{3,2,1,0:T(4,128)(2,1)S(1)} all-to-all(bf16[4,16,4,2048]{3,2,1,0:T(4,128)(2,1)S(1)} %bitcast.23), channel_id=1, replica_groups=mesh['dp'=8,'tz'=16,'ty'=4] {'ty'}, dimensions={0} | all-to-all | bytes 2097152 | tf_op jit(solution)/shard_map/all_to_all | solution.py:43
  22.4 0.7 reduce_sum.124
  23.1 32.5 %all_to_all.36 = bf16[16,4,2048]{2,1,0:T(4,128)(2,1)S(1)} all-to-all(bf16[16,4,2048]{2,1,0:T(4,128)(2,1)S(1)} %reduce_sum.124), channel_id=1, replica_groups=mesh['dp'=8,'tz'=16,'ty'=4] {'tz'}, dimensions={0} | all-to-all | bytes 524288 | tf_op jit(solution)/shard_map/all_to_all | solution.py:45
  56.5 22.5 %all_to_all.37 = bf16[16,4,2048]{2,1,0:T(4,128)(2,1)S(1)} all-to-all(bf16[16,4,2048]{2,1,0:T(4,128)(2,1)S(1)} %broadcast_in_dim.26), channel_id=1, replica_groups=mesh['dp'=8,'tz'=16,'ty'=4] {'tz'}, dimensions={0} | all-to-all | bytes 524288 | tf_op jit(solution)/shard_map/all_to_all | solution.py:48
  78.9 1.5 broadcast_in_dim.27
  80.4 3.6 %all-to-all-start.3 = ((bf16[4,16,4,2048]{3,2,1,0:T(4,128)(2,1)}), bf16[4,16,4,2048]{3,2,1,0:T(4,128)(2,1)S(1)}, u32[]{:S(2)}, u32[]{:S(2)}) async-start(bf16[4,16,4,2048]{3,2,1,0:T(4,128)(2,1)} %broadcast_in_dim.27), calls=%async_computation.3 | async-start | bytes 2097152 | tf_op jit(solution)/shard_map/all_to_all | solution.py:55
  84.1 10.9 %all-to-all-done.3 = bf16[4,16,4,2048]{3,2,1,0:T(4,128)(2,1)S(1)} async-done(((bf16[4,16,4,2048]{3,2,1,0:T(4,128)(2,1)}), bf16[4,16,4,2048]{3,2,1,0:T(4,128)(2,1)S(1)}, u32[]{:S(2)}, u32[]{:S(2)}) %all-to-all-start.3) | async-done | bytes 1048608 | tf_op jit(solution)/shard_map/all_to_all | solution.py:55
  95.0 3.6 %stack.26 = bf16[8,1952,256]{2,1,0:T(8,128)(2,1)} broadcast(bf16[1952,256]{1,0:T(8,128)(2,1)S(1)} %slice-done), dimensions={1,2} | broadcast | bytes 8994816 | tf_op jit(solution)/shard_map/stack | solution.py:11
  98.6 5.3 %all-to-all-start.4 = ((bf16[8,1952,256]{2,1,0:T(8,128)(2,1)}), bf16[8,1952,256]{2,1,0:T(8,128)(2,1)}, u32[]{:S(2)}, u32[]{:S(2)}) async-start(bf16[8,1952,256]{2,1,0:T(8,128)(2,1)} %stack.26), calls=%async_computation.4 | async-start | bytes 15990784 | tf_op jit(solution)/shard_map/all_to_all | solution.py:11
  103.9 89.1 %all-to-all-done.4 = bf16[8,1952,256]{2,1,0:T(8,128)(2,1)} async-done(((bf16[8,1952,256]{2,1,0:T(8,128)(2,1)}), bf16[8,1952,256]{2,1,0:T(8,128)(2,1)}, u32[]{:S(2)}, u32[]{:S(2)}) %all-to-all-start.4) | async-done | bytes 7995424 | tf_op jit(solution)/shard_map/all_to_all | solution.py:11
  193.0 3.7 %stack.63 = bf16[8,1968,256]{2,1,0:T(8,128)(2,1)} broadcast(bf16[1968,256]{1,0:T(8,128)(2,1)S(1)} %slice-done.1), dimensions={1,2} | broadcast | bytes 9068544 | tf_op jit(solution)/shard_map/stack | solution.py:11
  196.7 6.4 %all-to-all-start.5 = ((bf16[8,1968,256]{2,1,0:T(8,128)(2,1)}), bf16[8,1968,256]{2,1,0:T(8,128)(2,1)}, u32[]{:S(2)}, u32[]{:S(2)}) async-start(bf16[8,1968,256]{2,1,0:T(8,128)(2,1)} %stack.63), calls=%async_computation.5 | async-start | bytes 16121856 | tf_op jit(solution)/shard_map/all_to_all | solution.py:11
  203.7 1.1 reshape.142
  204.8 7.7 %copy.75 = bf16[8,244,8,256]{3,2,0,1:T(8,128)(2,1)} copy(bf16[8,244,8,256]{3,2,1,0:T(8,128)(2,1)} %bitcast.7) | data formatting | bytes 15990784 | tf_op jit(solution)/shard_map/reshape | solution.py:12
  212.5 5.6 %fusion.4 = (f32[256]{0:T(256)S(1)}, f32[256,1952]{0,1:T(8,128)S(1)}) fusion(bf16[256,2048]{1,0:T(8,128)(2,1)S(1)} %copy-done.2, bf16[1952,2048]{1,0:T(8,128)(2,1)} %bitcast.20), kind=kOutput, calls=%fused_computation.40 | convolution fusion | flops 2047319808 | bytes 11043840 | tf_op jit(solution)/shard_map/dot_general | solution.py:24
  219.5 73.4 %all-to-all-done.5 = bf16[8,1968,256]{2,1,0:T(8,128)(2,1)} async-done(((bf16[8,1968,256]{2,1,0:T(8,128)(2,1)}), bf16[8,1968,256]{2,1,0:T(8,128)(2,1)}, u32[]{:S(2)}, u32[]{:S(2)}) %all-to-all-start.5) | async-done | bytes 8060960 | tf_op jit(solution)/shard_map/all_to_all | solution.py:11
  292.8 7.7 %copy.76 = bf16[8,246,8,256]{3,2,0,1:T(8,128)(2,1)} copy(bf16[8,246,8,256]{3,2,1,0:T(8,128)(2,1)} %bitcast.9) | data formatting | bytes 16121856 | tf_op jit(solution)/shard_map/reshape | solution.py:12
  300.5 5.6 %fusion.3 = (f32[256]{0:T(256)S(1)}, f32[256,1968]{0,1:T(8,128)S(1)}) fusion(bf16[256,2048]{1,0:T(8,128)(2,1)S(1)} %copy-done.3, bf16[1968,2048]{1,0:T(8,128)(2,1)} %bitcast.19), kind=kOutput, calls=%fused_computation.39 | convolution fusion | flops 2064101120 | bytes 11125760 | tf_op jit(solution)/shard_map/dot_general | solution.py:24
  306.3 1.0 exponential_reduce_fusion
  308.0 0.9 copy.73
  308.9 9.9 %all-to-all-start.6 = ((f32[64,4,2,4]{1,3,2,0:T(4,128)}), f32[64,4,2,4]{1,3,2,0:T(4,128)S(1)}, u32[]{:S(2)}, u32[]{:S(2)}) async-start(f32[64,4,2,4]{1,3,2,0:T(4,128)} %copy.73), calls=%async_computation.6 | async-start | bytes 524288 | tf_op jit(solution)/shard_map/all_to_all | solution.py:86
  319.4 21.7 %all-to-all-done.6 = f32[64,4,2,4]{1,3,2,0:T(4,128)S(1)} async-done(((f32[64,4,2,4]{1,3,2,0:T(4,128)}), f32[64,4,2,4]{1,3,2,0:T(4,128)S(1)}, u32[]{:S(2)}, u32[]{:S(2)}) %all-to-all-start.6) | async-done | bytes 8224 | tf_op jit(solution)/shard_map/all_to_all | solution.py:86
  341.2 1.0 copy.74
  (56 shorter events, 7.2 us)
Async XLA Ops:
  0.6 1.1 copy-start
  3.1 53.2 %copy-start.4 = (f32[2048]{0:T(1024)S(1)}, f32[2048]{0:T(1024)}, u32[]{:S(2)}) copy-start(f32[2048]{0:T(1024)} %param.10) | copy-start | bytes 24580
  3.1 53.2 %copy-start.5 = (f32[2048]{0:T(1024)S(1)}, f32[2048]{0:T(1024)}, u32[]{:S(2)}) copy-start(f32[2048]{0:T(1024)} %param.9) | copy-start | bytes 24580
  80.4 14.5 %slice-start = ((bf16[3920,256]{1,0:T(8,128)(2,1)}), bf16[1952,256]{1,0:T(8,128)(2,1)S(1)}, s32[]{:S(2)}) async-start(bf16[3920,256]{1,0:T(8,128)(2,1)} %param.11), calls=%async_computation.7 | async-start | bytes 1998848 | tf_op jit(solution)/shard_map/slice | solution.py:68
  80.4 14.5 %all-to-all-start.3 = ((bf16[4,16,4,2048]{3,2,1,0:T(4,128)(2,1)}), bf16[4,16,4,2048]{3,2,1,0:T(4,128)(2,1)S(1)}, u32[]{:S(2)}, u32[]{:S(2)}) async-start(bf16[4,16,4,2048]{3,2,1,0:T(4,128)(2,1)} %broadcast_in_dim.27), calls=%async_computation.3 | async-start | bytes 2097152 | tf_op jit(solution)/shard_map/all_to_all | solution.py:55
  98.6 94.4 %all-to-all-start.4 = ((bf16[8,1952,256]{2,1,0:T(8,128)(2,1)}), bf16[8,1952,256]{2,1,0:T(8,128)(2,1)}, u32[]{:S(2)}, u32[]{:S(2)}) async-start(bf16[8,1952,256]{2,1,0:T(8,128)(2,1)} %stack.26), calls=%async_computation.4 | async-start | bytes 15990784 | tf_op jit(solution)/shard_map/all_to_all | solution.py:11
  103.9 89.1 %slice-start.1 = ((bf16[3920,256]{1,0:T(8,128)(2,1)}), bf16[1968,256]{1,0:T(8,128)(2,1)S(1)}, s32[]{:S(2)}) async-start(bf16[3920,256]{1,0:T(8,128)(2,1)} %param.11), calls=%async_computation.8 | async-start | bytes 2015232 | tf_op jit(solution)/shard_map/slice | solution.py:68
  196.7 6.4 %copy-start.7 = (s32[256]{0:T(256)S(1)}, s32[256]{0:T(256)}, u32[]{:S(2)}) copy-start(s32[256]{0:T(256)} %param.14) | copy-start | bytes 3076
  196.7 96.1 %all-to-all-start.5 = ((bf16[8,1968,256]{2,1,0:T(8,128)(2,1)}), bf16[8,1968,256]{2,1,0:T(8,128)(2,1)}, u32[]{:S(2)}, u32[]{:S(2)}) async-start(bf16[8,1968,256]{2,1,0:T(8,128)(2,1)} %stack.63), calls=%async_computation.5 | async-start | bytes 16121856 | tf_op jit(solution)/shard_map/all_to_all | solution.py:11
  204.8 7.7 %copy-start.2 = (bf16[256,2048]{1,0:T(8,128)(2,1)S(1)}, bf16[256,2048]{1,0:T(8,128)(2,1)}, u32[]{:S(2)}) copy-start(bf16[256,2048]{1,0:T(8,128)(2,1)} %reshape.142) | copy-start | bytes 3145732
  292.8 7.7 %copy-start.3 = (bf16[256,2048]{1,0:T(8,128)(2,1)S(1)}, bf16[256,2048]{1,0:T(8,128)(2,1)}, u32[]{:S(2)}) copy-start(bf16[256,2048]{1,0:T(8,128)(2,1)} %reshape.142) | copy-start | bytes 3145732
  306.3 37.9 %copy-start.1 = (bf16[128,2048]{1,0:T(8,128)(2,1)S(1)}, bf16[128,2048]{1,0:T(8,128)(2,1)}, u32[]{:S(2)}) copy-start(bf16[128,2048]{1,0:T(8,128)(2,1)} %param.8) | copy-start | bytes 1572868
  306.3 36.8 %copy-start.6 = (s32[256]{0:T(256)S(1)}, s32[256]{0:T(256)}, u32[]{:S(2)}) copy-start(s32[256]{0:T(256)} %param.13) | copy-start | bytes 3076
  306.3 36.8 %copy-start.8 = (s32[256]{0:T(256)S(1)}, s32[256]{0:T(256)}, u32[]{:S(2)}) copy-start(s32[256]{0:T(256)} %param.15) | copy-start | bytes 3076
  308.9 32.3 %all-to-all-start.6 = ((f32[64,4,2,4]{1,3,2,0:T(4,128)}), f32[64,4,2,4]{1,3,2,0:T(4,128)S(1)}, u32[]{:S(2)}, u32[]{:S(2)}) async-start(f32[64,4,2,4]{1,3,2,0:T(4,128)} %copy.73), calls=%async_computation.6 | async-start | bytes 524288 | tf_op jit(solution)/shard_map/all_to_all | solution.py:86
